TPU v7x, 256 devices: a whole 4x4x8 slice. The times are simulated.
256 devices in a mesh: req: 2 (over core), seq: 16 (over y, x), tp: 8 (over z).
Axes of the slice: x: 4, y: 4, z: 8, core: 2. Of those that a mesh axis runs over, the one named last changes fastest.
Arguments:
- queries: bfloat16 [4, 512, 3072], P('req', 'seq', 'tp'), may hold values from -48 to 48
- new_kv: bfloat16 [4, 512, 2, 3072], P('req', 'seq', None, 'tp'), may hold values from -4 to 4
- cache_kv: bfloat16 [4, 16384, 2, 3072], P('req', 'seq', None, 'tp'), may hold values from -4 to 4
- cached_len: int32 [4], P('req'), may hold values from 1 to 16384, as said below
- residual_in: bfloat16 [4, 512, 3072], P('req', 'seq', 'tp'), may hold values from -1.5 to 1.5
- norm_gain: float32 [3072], replicated, may hold values from 0.1 to 1.9
- gate_w: bfloat16 [3072, 4096], P(None, 'tp'), may hold values from -0.109375 to 0.109375
- up_w: bfloat16 [3072, 4096], P(None, 'tp'), may hold values from -0.109375 to 0.109375
- down_w: bfloat16 [4096, 3072], P('tp'), may hold values from -0.09375 to 0.09375
- owner: int32 [32, 64, 1], P(('req', 'seq')), may hold values from 0 to 31; in each aligned block of 64 rows (0 to 63, 64 to 127, ..., all dimensions but the last counted through in order) at most 4 rows name the same one
Outputs:
- layer_out: bfloat16 [32, 32, 4, 3072], P(('req', 'seq'), None, None, 'tp')
Inputs may be any that keep to these rules, and one draw needn't show every extreme that they name: `cached_len`: exactly 1 request have 16384 - 16384 // 8 cached positions or more, one of them exactly 16384; every other request has at most 1024. Within one row block no owner is named by more than 4 rows.
All inputs are finite; a program needn't handle non-finite values.
Results may differ from a plain program's by a relative error of at most 0.02.
Values may be sent and summed in bfloat16 or wider, within the bound.
No kernel may reach another device: no remote copies, remote signals or barrier semaphores. Data moves between devices by JAX's collectives and lax.ppermute only.
A program may use at most 256 MiB of HBM per device.

v0:
```python
import jax
import jax.numpy as jnp
from jax import lax
from jax.sharding import PartitionSpec as P

HEAD = 96
masked_floor = -1e30


def block_stats(query_heads, key_heads, value_heads, visible):
    scores = jnp.einsum(
        "qhd,khd->qhk", query_heads, key_heads, preferred_element_type=jnp.float32
    ) * HEAD ** (-0.5)
    visible_heads = visible[:, None, :]
    masked = jnp.where(visible_heads, scores, masked_floor)
    row_peak = jnp.max(masked, axis=-1)
    weights = jnp.where(visible_heads, jnp.exp(masked - row_peak[..., None]), 0.0)
    row_total = jnp.sum(weights, axis=-1)
    weighted = jnp.einsum(
        "qhk,khd->qhd",
        weights.astype(jnp.bfloat16),
        value_heads,
        preferred_element_type=jnp.float32,
    )
    return (row_peak, row_total, weighted.reshape(weighted.shape[0], -1))


def slot_partial(query_slot, cached_slot, fresh_slot, length, seq_index):
    query_count = query_slot.shape[0]
    head_count = query_slot.shape[1] // HEAD
    query_heads = query_slot.reshape(query_count, head_count, HEAD)
    positions = jnp.arange(query_count, dtype=jnp.int32)
    fresh_count = fresh_slot.shape[0]
    fresh_index = seq_index * fresh_count + jnp.arange(fresh_count, dtype=jnp.int32)
    fresh_visible = fresh_index[None, :] <= positions[:, None]
    shard_span = cached_slot.shape[0]
    shard_offset = seq_index * shard_span
    key_total = shard_span + fresh_count
    keys_all = jnp.concatenate([cached_slot[:, 0], fresh_slot[:, 0]], axis=0).reshape(
        key_total, head_count, HEAD
    )
    values_all = jnp.concatenate([cached_slot[:, 1], fresh_slot[:, 1]], axis=0).reshape(
        key_total, head_count, HEAD
    )
    cached_index = shard_offset + jnp.arange(shard_span, dtype=jnp.int32)
    cached_visible = jnp.broadcast_to((cached_index < length)[None, :], (query_count, shard_span))
    visible = jnp.concatenate([cached_visible, fresh_visible], axis=1)
    return block_stats(query_heads, keys_all, values_all, visible)


def normalize(features, norm_gain):
    values = features.astype(jnp.float32)
    mean_square = jnp.mean(values * values, axis=-1, keepdims=True)
    return (values * lax.rsqrt(mean_square + 1e-05) * norm_gain).astype(jnp.bfloat16)


def per_device(
    queries, new_kv, cache_kv, cached_len, residual_in, norm_gain, gate_w, up_w, down_w, owner
):
    slot_count, token_count, width_local = queries.shape
    seq_index = lax.axis_index("seq")
    all_queries = lax.all_gather(queries, "seq", axis=1, tiled=True)
    partials = [
        slot_partial(
            all_queries[slot_number],
            cache_kv[slot_number],
            new_kv[slot_number],
            cached_len[slot_number],
            seq_index,
        )
        for slot_number in range(slot_count)
    ]
    row_peak = jnp.stack([partial_item[0] for partial_item in partials])
    row_total = jnp.stack([partial_item[1] for partial_item in partials])
    weighted = jnp.stack([partial_item[2] for partial_item in partials])
    pieces = (
        lax.all_to_all(row_peak[None], "seq", split_axis=2, concat_axis=0, tiled=True),
        lax.all_to_all(row_total[None], "seq", split_axis=2, concat_axis=0, tiled=True),
        lax.all_to_all(weighted[None], "seq", split_axis=2, concat_axis=0, tiled=True),
    )
    source_peak, source_total, source_sum = pieces
    joint_peak = jnp.max(source_peak, axis=0)
    source_scale = jnp.exp(source_peak - joint_peak[None])
    own_total = jnp.sum(source_total * source_scale, axis=0)
    grouped = source_sum.reshape(source_sum.shape[:-1] + (source_peak.shape[-1], HEAD))
    own_sum = jnp.sum(grouped * source_scale[..., None], axis=0).reshape(source_sum.shape[1:])
    head_count = width_local // HEAD
    attention = (
        own_sum.reshape(slot_count, token_count, head_count, HEAD) / own_total[..., None]
    ).reshape(slot_count, token_count, width_local)
    stream = (residual_in.astype(jnp.float32) + attention).astype(jnp.bfloat16)
    stream_rows = stream.reshape(slot_count * token_count, width_local)
    owner_ids = owner.reshape(-1)
    owner_count = lax.axis_size(("req", "seq"))
    row_count = owner_ids.shape[0]
    slot_cap = max(2, 2 * row_count // owner_count)
    matches = (owner_ids[:, None] == jnp.arange(owner_count, dtype=jnp.int32)[None, :]).astype(
        jnp.int32
    )
    ranking = jnp.sum(jnp.cumsum(matches, axis=0) * matches, axis=1) - 1
    outgoing = (
        jnp.zeros((owner_count * slot_cap, width_local), jnp.bfloat16)
        .at[owner_ids * slot_cap + ranking]
        .set(stream_rows)
    )
    incoming = lax.all_to_all(
        outgoing.reshape(owner_count, slot_cap, width_local),
        ("req", "seq"),
        split_axis=0,
        concat_axis=0,
        tiled=True,
    )
    arrived = incoming.reshape(owner_count * slot_cap, width_local)
    full_rows = lax.all_gather(arrived, "tp", axis=1, tiled=True)
    normed = normalize(full_rows, norm_gain)
    gate_out = jnp.dot(normed, gate_w, preferred_element_type=jnp.float32)
    up_out = jnp.dot(normed, up_w, preferred_element_type=jnp.float32)
    hidden = (jax.nn.silu(gate_out) * up_out).astype(jnp.bfloat16)
    partial_sum = jnp.dot(hidden, down_w, preferred_element_type=jnp.float32)
    unit_share = lax.psum_scatter(
        partial_sum.astype(jnp.bfloat16), "tp", scatter_dimension=1, tiled=True
    ).astype(jnp.float32)
    result = (arrived.astype(jnp.float32) + unit_share).astype(jnp.bfloat16)
    return result.reshape(1, owner_count, slot_cap, width_local)


def solution(mesh):
    return jax.shard_map(
        per_device,
        mesh=mesh,
        in_specs=(
            P("req", "seq", "tp"),
            P("req", "seq", None, "tp"),
            P("req", "seq", None, "tp"),
            P("req"),
            P("req", "seq", "tp"),
            P(),
            P(None, "tp"),
            P(None, "tp"),
            P("tp", None),
            P(("req", "seq"), None, None),
        ),
        out_specs=P(("req", "seq"), None, None, "tp"),
        check_vma=False,
    )
```

profile of v0, /device:TPU:2, one launch (start us, length us, event | category | flops | bytes accessed | tf_op | source)
XLA Modules:
  0.0 262.6 jit_solution(4247062035156930165)
XLA Ops:
  13.7 24.4 %all_gather.6 = bf16[2,512,384]{2,1,0:T(8,128)(2,1)S(1)} all-gather(bf16[2,32,384]{2,1,0:T(8,128)(2,1)} %param.10), channel_id=1, replica_groups=mesh['req'=2,'seq'=16,'tp'=8] {'seq'}, dimensions={1}, use_global_device_ids=true | all-gather | bytes 835584 | tf_op jit(solution)/shard_map/all_gather | solution.py:62
  38.9 1.9 copy.57
  41.8 3.9 %slice_bitcast_fusion.1 = (bf16[1024,2,384]{2,1,0:T(2,128)(2,1)S(1)}, bf16[1024,2,384]{2,1,0:T(2,128)(2,1)S(1)}) fusion(bf16[2,1024,2,384]{3,2,1,0:T(2,128)(2,1)} %param.12), kind=kLoop, calls=%fused_computation.26 | loop fusion | bytes 6291456 | tf_op jit(solution)/shard_map/squeeze | solution.py:66
  45.6 6.3 %fusion.60 = (bf16[1024,1,384]{2,1,0:T(2,128)(2,1)}, bf16[1024,1,384]{2,1,0:T(2,128)(2,1)}, bf16[1024,1,384]{2,1,0:T(2,128)(2,1)}, bf16[1024,1,384]{2,1,0:T(2,128)(2,1)}) fusion(bf16[1024,2,384]{2,1,0:T(2,128)(2,1)S(1)} %get-tuple-element.7, bf16[1024,2,384]{2,1,0:T(2,128)(2,1)S(1)} %get-tuple-element.8), kind=kLoop, calls=%fused_computation.86 | loop fusion | bytes 6291456 | tf_op jit(solution)/shard_map/slice | solution.py:42
  51.9 4.7 %copy.55 = bf16[1024,1,384]{0,2,1:T(8,128)(2,1)} copy(bf16[1024,1,384]{2,1,0:T(2,128)(2,1)} %get-tuple-element.10) | data formatting | bytes 1572864 | tf_op jit(solution)/shard_map/slice | solution.py:39
  56.6 4.7 %copy.60 = bf16[1024,1,384]{0,2,1:T(8,128)(2,1)} copy(bf16[1024,1,384]{2,1,0:T(2,128)(2,1)} %get-tuple-element.33) | data formatting | bytes 1572864 | tf_op jit(solution)/shard_map/slice | solution.py:39
  63.2 6.7 %fusion.1 = (f32[512,4]{0,1:T(4,128)S(1)}, f32[4,1056,512]{2,1,0:T(8,128)}) fusion(pred[512,1056]{0,1:T(8,128)(4,1)S(1)} %get-tuple-element.22, bf16[512,4,96]{0,2,1:T(8,128)(2,1)S(1)} %bitcast.116, bf16[32,4,96]{0,2,1:T(8,128)(2,1)} %bitcast.118, bf16[1024,4,96]{0,2,1:T(8,128)(2,1)} %bitcast.114), kind=kOutput, calls=%fused_computation.6 | convolution fusion | flops 423344128 | bytes 10403840 | tf_op jit(solution)/shard_map/qhd,khd->qhk/dot_general | solution.py:11
  69.9 5.2 %fusion = (f32[512,4]{0,1:T(4,128)S(1)}, f32[4,1056,512]{2,1,0:T(8,128)}) fusion(pred[512,1056]{0,1:T(8,128)(4,1)S(1)} %get-tuple-element.21, bf16[512,4,96]{0,2,1:T(8,128)(2,1)S(1)} %bitcast.115, bf16[32,4,96]{0,2,1:T(8,128)(2,1)S(1)} %bitcast.117, bf16[1024,4,96]{0,2,1:T(8,128)(2,1)S(1)} %bitcast.112), kind=kOutput, calls=%fused_computation.5 | convolution fusion | flops 423344128 | bytes 10403840 | tf_op jit(solution)/shard_map/qhd,khd->qhk/dot_general | solution.py:11
  76.1 1.9 bitcast_bitcast_fusion.1
  78.0 2.4 reshape.128
  80.3 5.7 %all-to-all-start.1 = ((f32[16,1,256]{2,1,0:T(1,128)}), f32[16,1,256]{2,1,0:T(1,128)S(1)}, u32[]{:S(2)}, u32[]{:S(2)}) async-start(f32[16,1,256]{2,1,0:T(1,128)} %reshape.128), calls=%async_computation.1 | async-start | bytes 32768 | tf_op jit(solution)/shard_map/all_to_all | solution.py:77
  86.9 4.7 %copy.53 = bf16[1024,1,384]{0,2,1:T(8,128)(2,1)} copy(bf16[1024,1,384]{2,1,0:T(2,128)(2,1)} %get-tuple-element.9) | data formatting | bytes 1572864 | tf_op jit(solution)/shard_map/slice | solution.py:42
  91.6 4.7 %copy.58 = bf16[1024,1,384]{0,2,1:T(8,128)(2,1)} copy(bf16[1024,1,384]{2,1,0:T(2,128)(2,1)} %get-tuple-element.34) | data formatting | bytes 1572864 | tf_op jit(solution)/shard_map/slice | solution.py:42
  96.3 4.8 %fusion.4 = f32[512,4]{0,1:T(4,128)S(1)} fusion(f32[4,1056,512]{2,1,0:T(8,128)} %get-tuple-element.26, f32[512,4]{0,1:T(4,128)S(1)} %get-tuple-element.25, pred[512,1056]{0,1:T(8,128)(4,1)} %copy-done.7), kind=kLoop, calls=%fused_computation.9 | loop fusion | flops 10811392 | bytes 9207808 | tf_op jit(solution)/shard_map/reduce_sum | solution.py:18
  102.5 2.2 fusion.2
  105.7 7.5 %fusion.6 = f32[4,96,512]{2,1,0:T(8,128)} fusion(f32[4,1056,512]{2,1,0:T(8,128)} %get-tuple-element.26, f32[512,4]{0,1:T(4,128)S(1)} %get-tuple-element.25, pred[512,1056]{0,1:T(8,128)(4,1)} %copy-done.7, bf16[32,4,96]{0,2,1:T(8,128)(2,1)} %bitcast.120, bf16[1024,4,96]{0,2,1:T(8,128)(2,1)} %bitcast.113), kind=kOutput, calls=%fused_computation.11 | convolution fusion | flops 427671552 | bytes 10797056 | tf_op jit(solution)/shard_map/qhk,khd->qhd/dot_general | solution.py:19
  113.3 3.7 %fusion.8 = f32[4,96,512]{2,1,0:T(8,128)} fusion(f32[4,1056,512]{2,1,0:T(8,128)S(1)} %bitcast.104, f32[512,4]{0,1:T(4,128)S(1)} %get-tuple-element.27, pred[512,1056]{0,1:T(8,128)(4,1)S(1)} %copy-done.6, bf16[32,4,96]{0,2,1:T(8,128)(2,1)S(1)} %bitcast.119, bf16[1024,4,96]{0,2,1:T(8,128)(2,1)S(1)} %bitcast.111), kind=kOutput, calls=%fused_computation.12 | convolution fusion | flops 427671552 | bytes 10797056 | tf_op jit(solution)/shard_map/qhk,khd->qhd/dot_general | solution.py:19
  117.8 3.1 %copy.64 = f32[1,512,384]{2,0,1:T(1,128)} copy(f32[1,512,384]{1,2,0:T(8,128)} %bitcast.109) | data formatting | bytes 1572864 | tf_op jit(solution)/shard_map/stack;reshape | solution.py:75
  120.9 3.0 %copy.63 = f32[1,512,384]{2,0,1:T(1,128)} copy(f32[1,512,384]{1,2,0:T(8,128)} %bitcast.110) | data formatting | bytes 1572864 | tf_op jit(solution)/shard_map/stack;reshape | solution.py:75
  123.9 2.4 reshape.130
  126.3 7.2 %all-to-all-start.2 = ((f32[16,1,256]{2,1,0:T(1,128)}), f32[16,1,256]{2,1,0:T(1,128)S(1)}, u32[]{:S(2)}, u32[]{:S(2)}) async-start(f32[16,1,256]{2,1,0:T(1,128)} %reshape.130), calls=%async_computation.2 | async-start | bytes 32768 | tf_op jit(solution)/shard_map/all_to_all | solution.py:78
  133.5 3.9 %maximum_bitcast_fusion = f32[1,2,512,384]{3,1,0,2:T(2,128)} fusion(f32[1,512,384]{2,0,1:T(1,128)} %copy.64, f32[1,512,384]{2,0,1:T(1,128)} %copy.63), kind=kLoop, calls=%fused_computation.23 | loop fusion | flops 393216 | bytes 3145728 | tf_op jit(solution)/shard_map/broadcast_in_dim | solution.py:79
  137.4 2.3 all-to-all-done.2
  139.7 5.6 %all-to-all-start = ((f32[1,2,512,384]{3,1,0,2:T(2,128)}), f32[1,2,512,384]{3,1,0,2:T(2,128)}, u32[]{:S(2)}, u32[]{:S(2)}) async-start(f32[1,2,512,384]{3,1,0,2:T(2,128)} %maximum_bitcast_fusion), calls=%async_computation | async-start | bytes 3145728 | tf_op jit(solution)/shard_map/all_to_all | solution.py:79
  155.2 3.2 %mul.89 = f32[16,2,32,4,96]{4,3,2,0,1:T(4,128)} broadcast(f32[16,2,32,4]{3,2,0,1:T(8,128)} %copy.68), dimensions={0,1,2,3} | broadcast | bytes 1589248 | tf_op jit(solution)/shard_map/mul | solution.py:86
  158.4 3.2 %mul.90 = f32[16,1,2,32,384]{4,3,0,2,1:T(8,128)} reshape(f32[16,2,32,4,96]{4,3,2,0,1:T(4,128)} %mul.89) | data formatting | bytes 3145728 | tf_op jit(solution)/shard_map/mul | solution.py:86
  164.7 13.5 %all_to_all.56 = bf16[32,4,384]{2,1,0:T(4,128)(2,1)S(1)} all-to-all(bf16[32,4,384]{2,1,0:T(4,128)(2,1)S(1)} %reshape.111), channel_id=1, replica_groups=mesh['req'=2,'seq'=16,'tp'=8] {'req','seq'}, dimensions={0} | all-to-all | bytes 196608 | tf_op jit(solution)/shard_map/all_to_all | solution.py:106
  178.3 30.0 %all_gather.7 = bf16[128,3072]{1,0:T(8,128)(2,1)S(1)} all-gather(bf16[128,384]{1,0:T(8,128)(2,1)S(1)} %reshape.112), channel_id=1, replica_groups=mesh['req'=2,'seq'=16,'tp'=8] {'tp'}, dimensions={1}, use_global_device_ids=true | all-gather | bytes 884736 | tf_op jit(solution)/shard_map/all_gather | solution.py:114
  209.2 3.2 %fusion.37 = f32[128,512]{1,0:T(8,128)} fusion(bf16[3072,512]{1,0:T(8,128)(2,1)} %param.16, bf16[128,3072]{1,0:T(8,128)(2,1)S(1)} %all_gather.7, f32[3072]{0:T(1024)S(1)} %copy-done.18, f32[128]{0:T(128)S(1)} %add_rsqrt_fusion), kind=kOutput, calls=%fused_computation.48 | convolution fusion | flops 404226048 | bytes 4207104 | tf_op jit(solution)/shard_map/dot_general | solution.py:116
  212.4 4.2 %convolution_convert_fusion = bf16[128,3072]{1,0:T(8,128)(2,1)} fusion(bf16[512,3072]{1,0:T(8,128)(2,1)S(1)} %copy-done, bf16[3072,512]{1,0:T(8,128)(2,1)} %param.17, f32[128,512]{1,0:T(8,128)} %fusion.37, bf16[128,3072]{1,0:T(8,128)(2,1)} %copy-done.3, f32[3072]{0:T(1024)S(1)} %copy-done.18, f32[128]{0:T(128)S(1)} %add_rsqrt_fusion), kind=kOutput, calls=%fused_computation.15 | convolution fusion | flops 807665664 | bytes 8139264 | tf_op jit(solution)/shard_map/dot_general | solution.py:119
  216.6 2.3 copy.72
  218.9 35.1 %reduce-scatter.4.cloned.1.call-done = bf16[384,128]{1,0:T(8,128)(2,1)} async-done(((bf16[3072,128]{1,0:T(8,128)(2,1)}), bf16[384,128]{1,0:T(8,128)(2,1)}) %reduce-scatter.4.cloned.1.call-update) | async-done | bytes 98320
  (97 shorter events, 31.5 us)
Async XLA Ops:
  6.5 205.9 %copy-start = (bf16[512,3072]{1,0:T(8,128)(2,1)S(1)}, bf16[512,3072]{1,0:T(8,128)(2,1)}, u32[]{:S(2)}) copy-start(bf16[512,3072]{1,0:T(8,128)(2,1)} %param.18) | copy-start | bytes 9437188
  51.9 11.2 %copy-start.12 = (bf16[1,512,384]{1,2,0:T(8,128)(2,1)S(1)}, bf16[1,512,384]{1,2,0:T(8,128)(2,1)}, u32[]{:S(2)}) copy-start(bf16[1,512,384]{1,2,0:T(8,128)(2,1)} %copy.62) | copy-start | bytes 1179652
  63.1 6.8 %copy-start.7 = (pred[512,1056]{0,1:T(8,128)(4,1)}, pred[512,1056]{0,1:T(8,128)(4,1)S(1)}, u32[]{:S(2)}) copy-start(pred[512,1056]{0,1:T(8,128)(4,1)S(1)} %get-tuple-element.22) | copy-start | bytes 1622020
  63.1 6.8 %copy-start.4 = (pred[512,1056]{0,1:T(8,128)(4,1)}, pred[512,1056]{0,1:T(8,128)(4,1)S(1)}, u32[]{:S(2)}) copy-start(pred[512,1056]{0,1:T(8,128)(4,1)S(1)} %get-tuple-element.21) | copy-start | bytes 1622020
  63.1 6.7 %copy-start.10 = (bf16[1024,1,384]{0,2,1:T(8,128)(2,1)S(1)}, bf16[1024,1,384]{0,2,1:T(8,128)(2,1)}, u32[]{:S(2)}) copy-start(bf16[1024,1,384]{0,2,1:T(8,128)(2,1)} %copy.55) | copy-start | bytes 2359300
  63.1 6.7 %copy-start.11 = (bf16[1,512,384]{1,2,0:T(8,128)(2,1)S(1)}, bf16[1,512,384]{1,2,0:T(8,128)(2,1)}, u32[]{:S(2)}) copy-start(bf16[1,512,384]{1,2,0:T(8,128)(2,1)} %copy.57) | copy-start | bytes 1179652
  63.1 6.7 %copy-start.15 = (bf16[32,1,384]{0,2,1:T(8,128)(2,1)S(1)}, bf16[32,1,384]{0,2,1:T(8,128)(2,1)}, u32[]{:S(2)}) copy-start(bf16[32,1,384]{0,2,1:T(8,128)(2,1)} %copy.56) | copy-start | bytes 73732
  69.9 16.1 %copy-start.14 = (bf16[32,1,384]{2,1,0:T(2,128)(2,1)S(1)}, bf16[32,1,384]{2,1,0:T(2,128)(2,1)}, u32[]{:S(2)}) copy-start(bf16[32,1,384]{2,1,0:T(2,128)(2,1)} %get-tuple-element.17) | copy-start | bytes 73732
  69.9 16.3 %copy-start.13 = (bf16[32,1,384]{2,1,0:T(2,128)(2,1)S(1)}, bf16[32,1,384]{2,1,0:T(2,128)(2,1)}, u32[]{:S(2)}) copy-start(bf16[32,1,384]{2,1,0:T(2,128)(2,1)} %get-tuple-element.32) | copy-start | bytes 73732
  80.3 45.9 %all-to-all-start.1 = ((f32[16,1,256]{2,1,0:T(1,128)}), f32[16,1,256]{2,1,0:T(1,128)S(1)}, u32[]{:S(2)}, u32[]{:S(2)}) async-start(f32[16,1,256]{2,1,0:T(1,128)} %reshape.128), calls=%async_computation.1 | async-start | bytes 32768 | tf_op jit(solution)/shard_map/all_to_all | solution.py:77
  96.3 6.1 %copy-start.1 = (f32[4,1056,512]{2,1,0:T(8,128)S(1)}, f32[4,1056,512]{2,1,0:T(8,128)}, u32[]{:S(2)}) copy-start(f32[4,1056,512]{2,1,0:T(8,128)} %get-tuple-element.28) | copy-start | bytes 25952260
  96.3 6.2 %copy-start.5 = (pred[512,1056]{0,1:T(8,128)(4,1)S(1)}, pred[512,1056]{0,1:T(8,128)(4,1)}, u32[]{:S(2)}) copy-start(pred[512,1056]{0,1:T(8,128)(4,1)} %copy-done.4) | copy-start | bytes 1622020
  104.6 8.6 %slice-start = ((s8[8650752]{0:T(1024)(128)(4,1)}), s8[262144]{0:T(1024)(128)(4,1)S(1)}, s32[]{:S(2)}) async-start(s8[8650752]{0:T(1024)(128)(4,1)} %bitcast.103), calls=%async_computation.6 | async-start | bytes 524288
  105.7 7.5 %slice-start.1 = ((s8[8650752]{0:T(1024)(128)(4,1)}), s8[4194304]{0:T(1024)(128)(4,1)S(1)}, s32[]{:S(2)}) async-start(s8[8650752]{0:T(1024)(128)(4,1)} %bitcast.103), calls=%async_computation.7 | async-start | bytes 8388608
  105.7 7.5 %slice-start.2 = ((s8[8650752]{0:T(1024)(128)(4,1)}), s8[4194304]{0:T(1024)(128)(4,1)S(1)}, s32[]{:S(2)}) async-start(s8[8650752]{0:T(1024)(128)(4,1)} %bitcast.103), calls=%async_computation.8 | async-start | bytes 8388608
  105.7 7.5 %copy-start.6 = (pred[512,1056]{0,1:T(8,128)(4,1)S(1)}, pred[512,1056]{0,1:T(8,128)(4,1)}, u32[]{:S(2)}) copy-start(pred[512,1056]{0,1:T(8,128)(4,1)} %copy-done.4) | copy-start | bytes 1622020
  105.7 7.5 %copy-start.9 = (bf16[1024,1,384]{0,2,1:T(8,128)(2,1)S(1)}, bf16[1024,1,384]{0,2,1:T(8,128)(2,1)}, u32[]{:S(2)}) copy-start(bf16[1024,1,384]{0,2,1:T(8,128)(2,1)} %copy.53) | copy-start | bytes 2359300
  113.2 3.7 %copy-start.8 = (f32[2,512,4]{2,0,1:T(2,128)S(1)}, f32[2,512,4]{2,0,1:T(2,128)}, u32[]{:S(2)}) copy-start(f32[2,512,4]{2,0,1:T(2,128)} %copy.69) | copy-start | bytes 49156
  126.3 13.5 %all-to-all-start.2 = ((f32[16,1,256]{2,1,0:T(1,128)}), f32[16,1,256]{2,1,0:T(1,128)S(1)}, u32[]{:S(2)}, u32[]{:S(2)}) async-start(f32[16,1,256]{2,1,0:T(1,128)} %reshape.130), calls=%async_computation.2 | async-start | bytes 32768 | tf_op jit(solution)/shard_map/all_to_all | solution.py:78
  133.5 12.1 %copy-start.17 = (s32[1,64,1]{1,2,0:T(1,128)S(1)}, s32[1,64,1]{1,2,0:T(1,128)}, u32[]{:S(2)}) copy-start(s32[1,64,1]{1,2,0:T(1,128)} %param.19) | copy-start | bytes 772
  139.7 21.9 %all-to-all-start = ((f32[1,2,512,384]{3,1,0,2:T(2,128)}), f32[1,2,512,384]{3,1,0,2:T(2,128)}, u32[]{:S(2)}, u32[]{:S(2)}) async-start(f32[1,2,512,384]{3,1,0,2:T(2,128)} %maximum_bitcast_fusion), calls=%async_computation | async-start | bytes 3145728 | tf_op jit(solution)/shard_map/all_to_all | solution.py:79
  145.3 108.8 %reduce-scatter.4.cloned.1.call-start = ((), (), s32[]{:S(2)}) async-start(), calls=%async_computation.5 | async-start | bytes 884736
  161.6 2.2 copy-start.16
  161.6 1.9 copy-start.2
  163.3 45.9 %copy-start.18 = (f32[3072]{0:T(1024)S(1)}, f32[3072]{0:T(1024)}, u32[]{:S(2)}) copy-start(f32[3072]{0:T(1024)} %param.15) | copy-start | bytes 36868
  208.3 0.9 copy-start.3
Sparse Core Ops, SparseCore 0:
  219.1 34.9 reduce-scatter.3
where the time goes:
time: 264 us; the launch traced here: 263 us
  local copies, waits for them, and re-layouts  77.8 us (29%)
  blocking collectives  67.9 us (26%)
  waiting for transfers between devices  37.4 us (14%)
  matrix products  30.5 us (12%)
  starting transfers between devices  18.7 us (7%)
  other arithmetic  16.4 us (6%)
  between operations  13.7 us (5%)
    unnamed x2, waiting for transfers between devices  35.1 us
    all_gather x1, blocking collectives, per_device(): full_rows = lax.all_gather(arrived, 'tp', axis=1, tiled=True)  30 us
    all_gather x1, blocking collectives, per_device(): all_queries = lax.all_gather(queries, 'seq', axis=1, tiled=True)  24.4 us
    unnamed x52, local copies, waits for them, and re-layouts  16.3 us
    slice x3, local copies, waits for them, and re-layouts, slot_partial(): cached_slot[:, 1]  15.6 us
    all_to_all x1, blocking collectives, per_device(): lax.all_to_all(outgoing.reshape(owner_count, slot_cap, width_local), ('re...  13.5 us
    dot_general x2, matrix products, block_stats(): jnp.einsum('qhd,khd->qhk', query_heads, key_heads, preferred_element_type...  11.9 us
    dot_general x2, matrix products, block_stats(): jnp.einsum('qhk,khd->qhd', weights.astype(jnp.bfloat16), value_heads, pre...  11.2 us
  transfers between devices with their start and end apart: 4, of which 2 were waited for; matrix products, arithmetic and copies ran while one was open for 22% of the time, Pallas kernels for 0%

commit v1 on v0

--- a/solution.py
+++ b/solution.py
@@ -1,3 +1,4 @@
+import functools
 import jax
 import jax.numpy as jnp
 from jax import lax
@@ -5,6 +6,22 @@
 
 HEAD = 96
 masked_floor = -1e30
+
+
+def prepare_the_table(obj, d0, ndim_at):
+    side_arr = jnp.concatenate(
+        lax.all_to_all(
+            jnp.stack(jnp.split(obj, lax.axis_size("seq"), axis=d0)),
+            axis_name="seq",
+            split_axis=0,
+            concat_axis=0,
+        ),
+        axis=ndim_at,
+    )
+    return side_arr
+
+
+rounds_choose = functools.partial(prepare_the_table, d0=2, ndim_at=0)
 
 
 def block_stats(query_heads, key_heads, value_heads, visible):
@@ -74,7 +91,7 @@
     row_total = jnp.stack([partial_item[1] for partial_item in partials])
     weighted = jnp.stack([partial_item[2] for partial_item in partials])
     pieces = (
-        lax.all_to_all(row_peak[None], "seq", split_axis=2, concat_axis=0, tiled=True),
+        rounds_choose(row_peak[None]),
         lax.all_to_all(row_total[None], "seq", split_axis=2, concat_axis=0, tiled=True),
         lax.all_to_all(weighted[None], "seq", split_axis=2, concat_axis=0, tiled=True),
     )

time: 264 us -> 258 us (0.977)
  local copies, waits for them, and re-layouts: 77.8 us -> 71.4 us
    unnamed x52 -> x66, local copies, waits for them, and re-layouts: 16.3 us -> 12.1 us
  transfers between devices with their start and end apart: 4 -> 4, of which waited for: 2 -> 3; matrix products, arithmetic and copies ran while one was open for 22% -> 22% of each run, Pallas kernels for 0% -> 0%
where the time goes in v1:
time: 258 us; the launch traced here: 257 us
  local copies, waits for them, and re-layouts  71.4 us (28%)
  blocking collectives  66.5 us (26%)
  waiting for transfers between devices  39.6 us (15%)
  matrix products  30.5 us (12%)
  starting transfers between devices  18.7 us (7%)
  other arithmetic  16.4 us (6%)
  between operations  13.8 us (5%)
    unnamed x2, waiting for transfers between devices  35.1 us
    all_gather x1, blocking collectives, per_device(): full_rows = lax.all_gather(arrived, 'tp', axis=1, tiled=True)  30 us
    all_gather x1, blocking collectives, per_device(): all_queries = lax.all_gather(queries, 'seq', axis=1, tiled=True)  24.4 us
    slice x3, local copies, waits for them, and re-layouts, slot_partial(): cached_slot[:, 1]  15.6 us
    unnamed x66, local copies, waits for them, and re-layouts  12.1 us
    all_to_all x1, blocking collectives, per_device(): lax.all_to_all(outgoing.reshape(owner_count, slot_cap, width_local), ('re...  12.1 us
    dot_general x2, matrix products, block_stats(): jnp.einsum('qhd,khd->qhk', query_heads, key_heads, preferred_element_type...  11.9 us
    dot_general x2, matrix products, block_stats(): jnp.einsum('qhk,khd->qhd', weights.astype(jnp.bfloat16), value_heads, pre...  11.2 us
  transfers between devices with their start and end apart: 4, of which 3 were waited for; matrix products, arithmetic and copies ran while one was open for 22% of the time, Pallas kernels for 0%

profile of v1, /device:TPU:2, one launch (start us, length us, event | category | flops | bytes accessed | tf_op | source)
XLA Modules:
  0.0 257.0 jit_solution(1888843541305301346)
XLA Ops:
  13.7 24.4 %all_gather.6 = bf16[2,512,384]{2,1,0:T(8,128)(2,1)S(1)} all-gather(bf16[2,32,384]{2,1,0:T(8,128)(2,1)} %param.10), channel_id=1, replica_groups=mesh['req'=2,'seq'=16,'tp'=8] {'seq'}, dimensions={1}, use_global_device_ids=true | all-gather | bytes 835584 | tf_op jit(solution)/shard_map/all_gather | solution.py:79
  38.9 1.9 copy.71
  41.8 3.9 %slice_bitcast_fusion.1 = (bf16[1024,2,384]{2,1,0:T(2,128)(2,1)S(1)}, bf16[1024,2,384]{2,1,0:T(2,128)(2,1)S(1)}) fusion(bf16[2,1024,2,384]{3,2,1,0:T(2,128)(2,1)} %param.12), kind=kLoop, calls=%fused_computation.26 | loop fusion | bytes 6291456 | tf_op jit(solution)/shard_map/squeeze | solution.py:83
  45.6 6.3 %fusion.60 = (bf16[1024,1,384]{2,1,0:T(2,128)(2,1)}, bf16[1024,1,384]{2,1,0:T(2,128)(2,1)}, bf16[1024,1,384]{2,1,0:T(2,128)(2,1)}, bf16[1024,1,384]{2,1,0:T(2,128)(2,1)}) fusion(bf16[1024,2,384]{2,1,0:T(2,128)(2,1)S(1)} %get-tuple-element.7, bf16[1024,2,384]{2,1,0:T(2,128)(2,1)S(1)} %get-tuple-element.8), kind=kLoop, calls=%fused_computation.117 | loop fusion | bytes 6291456 | tf_op jit(solution)/shard_map/slice | solution.py:59
  51.9 4.7 %copy.69 = bf16[1024,1,384]{0,2,1:T(8,128)(2,1)} copy(bf16[1024,1,384]{2,1,0:T(2,128)(2,1)} %get-tuple-element.10) | data formatting | bytes 1572864 | tf_op jit(solution)/shard_map/slice | solution.py:56
  56.6 4.7 %copy.74 = bf16[1024,1,384]{0,2,1:T(8,128)(2,1)} copy(bf16[1024,1,384]{2,1,0:T(2,128)(2,1)} %get-tuple-element.33) | data formatting | bytes 1572864 | tf_op jit(solution)/shard_map/slice | solution.py:56
  61.3 1.8 pad_add_fusion.1
  63.2 6.7 %fusion.1 = (f32[512,4]{0,1:T(4,128)S(1)}, f32[4,1056,512]{2,1,0:T(8,128)}) fusion(pred[512,1056]{0,1:T(8,128)(4,1)S(1)} %get-tuple-element.22, bf16[512,4,96]{0,2,1:T(8,128)(2,1)S(1)} %bitcast.176, bf16[32,4,96]{0,2,1:T(8,128)(2,1)} %bitcast.178, bf16[1024,4,96]{0,2,1:T(8,128)(2,1)} %bitcast.173), kind=kOutput, calls=%fused_computation.6 | convolution fusion | flops 423344128 | bytes 10403840 | tf_op jit(solution)/shard_map/qhd,khd->qhk/dot_general | solution.py:28
  69.9 5.2 %fusion = (f32[512,4]{0,1:T(4,128)S(1)}, f32[4,1056,512]{2,1,0:T(8,128)}) fusion(pred[512,1056]{0,1:T(8,128)(4,1)S(1)} %get-tuple-element.21, bf16[512,4,96]{0,2,1:T(8,128)(2,1)S(1)} %bitcast.175, bf16[32,4,96]{0,2,1:T(8,128)(2,1)S(1)} %bitcast.177, bf16[1024,4,96]{0,2,1:T(8,128)(2,1)S(1)} %bitcast.171), kind=kOutput, calls=%fused_computation.5 | convolution fusion | flops 423344128 | bytes 10403840 | tf_op jit(solution)/shard_map/qhd,khd->qhk/dot_general | solution.py:28
  76.8 5.7 %all-to-all-start.1 = ((f32[16,1,256]{2,1,0:T(1,128)}), f32[16,1,256]{2,1,0:T(1,128)S(1)}, u32[]{:S(2)}, u32[]{:S(2)}) async-start(f32[16,1,256]{2,1,0:T(1,128)} %reshape.132), calls=%async_computation.1 | async-start | bytes 32768 | tf_op jit(solution)/shard_map/all_to_all | solution.py:13
  83.4 4.7 %copy.67 = bf16[1024,1,384]{0,2,1:T(8,128)(2,1)} copy(bf16[1024,1,384]{2,1,0:T(2,128)(2,1)} %get-tuple-element.9) | data formatting | bytes 1572864 | tf_op jit(solution)/shard_map/slice | solution.py:59
  88.0 4.7 %copy.72 = bf16[1024,1,384]{0,2,1:T(8,128)(2,1)} copy(bf16[1024,1,384]{2,1,0:T(2,128)(2,1)} %get-tuple-element.34) | data formatting | bytes 1572864 | tf_op jit(solution)/shard_map/slice | solution.py:59
  92.7 4.8 %fusion.4 = f32[512,4]{0,1:T(4,128)S(1)} fusion(f32[4,1056,512]{2,1,0:T(8,128)} %get-tuple-element.26, f32[512,4]{0,1:T(4,128)S(1)} %get-tuple-element.25, pred[512,1056]{0,1:T(8,128)(4,1)} %copy-done.7), kind=kLoop, calls=%fused_computation.9 | loop fusion | flops 10811392 | bytes 9207808 | tf_op jit(solution)/shard_map/reduce_sum | solution.py:35
  98.9 2.2 fusion.2
  102.2 7.5 %fusion.6 = f32[4,96,512]{2,1,0:T(8,128)} fusion(f32[4,1056,512]{2,1,0:T(8,128)} %get-tuple-element.26, f32[512,4]{0,1:T(4,128)S(1)} %get-tuple-element.25, pred[512,1056]{0,1:T(8,128)(4,1)} %copy-done.7, bf16[32,4,96]{0,2,1:T(8,128)(2,1)} %bitcast.180, bf16[1024,4,96]{0,2,1:T(8,128)(2,1)} %bitcast.172), kind=kOutput, calls=%fused_computation.11 | convolution fusion | flops 427671552 | bytes 10797056 | tf_op jit(solution)/shard_map/qhk,khd->qhd/dot_general | solution.py:36
  109.7 3.7 %fusion.8 = f32[4,96,512]{2,1,0:T(8,128)} fusion(f32[4,1056,512]{2,1,0:T(8,128)S(1)} %bitcast.164, f32[512,4]{0,1:T(4,128)S(1)} %get-tuple-element.27, pred[512,1056]{0,1:T(8,128)(4,1)S(1)} %copy-done.6, bf16[32,4,96]{0,2,1:T(8,128)(2,1)S(1)} %bitcast.179, bf16[1024,4,96]{0,2,1:T(8,128)(2,1)S(1)} %bitcast.170), kind=kOutput, calls=%fused_computation.12 | convolution fusion | flops 427671552 | bytes 10797056 | tf_op jit(solution)/shard_map/qhk,khd->qhd/dot_general | solution.py:36
  114.3 3.1 %copy.78 = f32[1,512,384]{2,0,1:T(1,128)} copy(f32[1,512,384]{1,2,0:T(8,128)} %bitcast.168) | data formatting | bytes 1572864 | tf_op jit(solution)/shard_map/stack;reshape | solution.py:92
  117.3 3.0 %copy.77 = f32[1,512,384]{2,0,1:T(1,128)} copy(f32[1,512,384]{1,2,0:T(8,128)} %bitcast.169) | data formatting | bytes 1572864 | tf_op jit(solution)/shard_map/stack;reshape | solution.py:92
  120.4 2.4 reshape.134
  122.7 7.2 %all-to-all-start.2 = ((f32[16,1,256]{2,1,0:T(1,128)}), f32[16,1,256]{2,1,0:T(1,128)S(1)}, u32[]{:S(2)}, u32[]{:S(2)}) async-start(f32[16,1,256]{2,1,0:T(1,128)} %reshape.134), calls=%async_computation.2 | async-start | bytes 32768 | tf_op jit(solution)/shard_map/all_to_all | solution.py:95
  130.0 3.9 %maximum_bitcast_fusion = f32[1,2,512,384]{3,1,0,2:T(2,128)} fusion(f32[1,512,384]{2,0,1:T(1,128)} %copy.78, f32[1,512,384]{2,0,1:T(1,128)} %copy.77), kind=kLoop, calls=%fused_computation.23 | loop fusion | flops 393216 | bytes 3145728 | tf_op jit(solution)/shard_map/broadcast_in_dim | solution.py:96
  133.9 2.3 all-to-all-done.2
  136.2 5.6 %all-to-all-start = ((f32[1,2,512,384]{3,1,0,2:T(2,128)}), f32[1,2,512,384]{3,1,0,2:T(2,128)}, u32[]{:S(2)}, u32[]{:S(2)}) async-start(f32[1,2,512,384]{3,1,0,2:T(2,128)} %maximum_bitcast_fusion), calls=%async_computation | async-start | bytes 3145728 | tf_op jit(solution)/shard_map/all_to_all | solution.py:96
  148.9 3.2 %mul.89 = f32[16,2,32,4,96]{4,3,2,0,1:T(4,128)} broadcast(f32[16,2,32,4]{3,2,0,1:T(8,128)} %copy.81), dimensions={0,1,2,3} | broadcast | bytes 1589248 | tf_op jit(solution)/shard_map/mul | solution.py:103
  152.1 3.2 %mul.90 = f32[16,1,2,32,384]{4,3,0,2,1:T(8,128)} reshape(f32[16,2,32,4,96]{4,3,2,0,1:T(4,128)} %mul.89) | data formatting | bytes 3145728 | tf_op jit(solution)/shard_map/mul | solution.py:103
  155.3 2.3 all-to-all-done
  160.6 12.1 %all_to_all.43 = bf16[32,4,384]{2,1,0:T(4,128)(2,1)S(1)} all-to-all(bf16[32,4,384]{2,1,0:T(4,128)(2,1)S(1)} %reshape.115), channel_id=1, replica_groups=mesh['req'=2,'seq'=16,'tp'=8] {'req','seq'}, dimensions={0} | all-to-all | bytes 196608 | tf_op jit(solution)/shard_map/all_to_all | solution.py:123
  172.7 30.0 %all_gather.7 = bf16[128,3072]{1,0:T(8,128)(2,1)S(1)} all-gather(bf16[128,384]{1,0:T(8,128)(2,1)S(1)} %reshape.116), channel_id=1, replica_groups=mesh['req'=2,'seq'=16,'tp'=8] {'tp'}, dimensions={1}, use_global_device_ids=true | all-gather | bytes 884736 | tf_op jit(solution)/shard_map/all_gather | solution.py:131
  203.7 3.2 %fusion.37 = f32[128,512]{1,0:T(8,128)} fusion(bf16[3072,512]{1,0:T(8,128)(2,1)} %param.16, bf16[128,3072]{1,0:T(8,128)(2,1)S(1)} %all_gather.7, f32[3072]{0:T(1024)S(1)} %copy-done.18, f32[128]{0:T(128)S(1)} %add_rsqrt_fusion), kind=kOutput, calls=%fused_computation.48 | convolution fusion | flops 404226048 | bytes 4207104 | tf_op jit(solution)/shard_map/dot_general | solution.py:133
  206.9 4.2 %convolution_convert_fusion = bf16[128,3072]{1,0:T(8,128)(2,1)} fusion(bf16[512,3072]{1,0:T(8,128)(2,1)S(1)} %copy-done, bf16[3072,512]{1,0:T(8,128)(2,1)} %param.17, f32[128,512]{1,0:T(8,128)} %fusion.37, bf16[128,3072]{1,0:T(8,128)(2,1)} %copy-done.3, f32[3072]{0:T(1024)S(1)} %copy-done.18, f32[128]{0:T(128)S(1)} %add_rsqrt_fusion), kind=kOutput, calls=%fused_computation.15 | convolution fusion | flops 807665664 | bytes 8139264 | tf_op jit(solution)/shard_map/dot_general | solution.py:136
  211.1 2.3 copy.86
  213.4 35.0 %reduce-scatter.4.cloned.1.call-done = bf16[384,128]{1,0:T(8,128)(2,1)} async-done(((bf16[3072,128]{1,0:T(8,128)(2,1)}), bf16[384,128]{1,0:T(8,128)(2,1)}) %reduce-scatter.4.cloned.1.call-update) | async-done | bytes 98320
  (110 shorter events, 27.5 us)
Async XLA Ops:
  6.5 200.3 %copy-start = (bf16[512,3072]{1,0:T(8,128)(2,1)S(1)}, bf16[512,3072]{1,0:T(8,128)(2,1)}, u32[]{:S(2)}) copy-start(bf16[512,3072]{1,0:T(8,128)(2,1)} %param.18) | copy-start | bytes 9437188
  51.9 11.2 %copy-start.12 = (bf16[1,512,384]{1,2,0:T(8,128)(2,1)S(1)}, bf16[1,512,384]{1,2,0:T(8,128)(2,1)}, u32[]{:S(2)}) copy-start(bf16[1,512,384]{1,2,0:T(8,128)(2,1)} %copy.76) | copy-start | bytes 1179652
  63.1 6.8 %copy-start.7 = (pred[512,1056]{0,1:T(8,128)(4,1)}, pred[512,1056]{0,1:T(8,128)(4,1)S(1)}, u32[]{:S(2)}) copy-start(pred[512,1056]{0,1:T(8,128)(4,1)S(1)} %get-tuple-element.22) | copy-start | bytes 1622020
  63.1 6.8 %copy-start.4 = (pred[512,1056]{0,1:T(8,128)(4,1)}, pred[512,1056]{0,1:T(8,128)(4,1)S(1)}, u32[]{:S(2)}) copy-start(pred[512,1056]{0,1:T(8,128)(4,1)S(1)} %get-tuple-element.21) | copy-start | bytes 1622020
  63.1 6.7 %copy-start.10 = (bf16[1024,1,384]{0,2,1:T(8,128)(2,1)S(1)}, bf16[1024,1,384]{0,2,1:T(8,128)(2,1)}, u32[]{:S(2)}) copy-start(bf16[1024,1,384]{0,2,1:T(8,128)(2,1)} %copy.69) | copy-start | bytes 2359300
  63.1 6.7 %copy-start.11 = (bf16[1,512,384]{1,2,0:T(8,128)(2,1)S(1)}, bf16[1,512,384]{1,2,0:T(8,128)(2,1)}, u32[]{:S(2)}) copy-start(bf16[1,512,384]{1,2,0:T(8,128)(2,1)} %copy.71) | copy-start | bytes 1179652
  63.1 6.7 %copy-start.15 = (bf16[32,1,384]{0,2,1:T(8,128)(2,1)S(1)}, bf16[32,1,384]{0,2,1:T(8,128)(2,1)}, u32[]{:S(2)}) copy-start(bf16[32,1,384]{0,2,1:T(8,128)(2,1)} %copy.70) | copy-start | bytes 73732
  69.9 12.6 %copy-start.14 = (bf16[32,1,384]{2,1,0:T(2,128)(2,1)S(1)}, bf16[32,1,384]{2,1,0:T(2,128)(2,1)}, u32[]{:S(2)}) copy-start(bf16[32,1,384]{2,1,0:T(2,128)(2,1)} %get-tuple-element.17) | copy-start | bytes 73732
  69.9 12.7 %copy-start.13 = (bf16[32,1,384]{2,1,0:T(2,128)(2,1)S(1)}, bf16[32,1,384]{2,1,0:T(2,128)(2,1)}, u32[]{:S(2)}) copy-start(bf16[32,1,384]{2,1,0:T(2,128)(2,1)} %get-tuple-element.32) | copy-start | bytes 73732
  76.8 45.9 %all-to-all-start.1 = ((f32[16,1,256]{2,1,0:T(1,128)}), f32[16,1,256]{2,1,0:T(1,128)S(1)}, u32[]{:S(2)}, u32[]{:S(2)}) async-start(f32[16,1,256]{2,1,0:T(1,128)} %reshape.132), calls=%async_computation.1 | async-start | bytes 32768 | tf_op jit(solution)/shard_map/all_to_all | solution.py:13
  92.7 6.1 %copy-start.1 = (f32[4,1056,512]{2,1,0:T(8,128)S(1)}, f32[4,1056,512]{2,1,0:T(8,128)}, u32[]{:S(2)}) copy-start(f32[4,1056,512]{2,1,0:T(8,128)} %get-tuple-element.28) | copy-start | bytes 25952260
  92.7 6.2 %copy-start.5 = (pred[512,1056]{0,1:T(8,128)(4,1)S(1)}, pred[512,1056]{0,1:T(8,128)(4,1)}, u32[]{:S(2)}) copy-start(pred[512,1056]{0,1:T(8,128)(4,1)} %copy-done.4) | copy-start | bytes 1622020
  101.1 8.6 %slice-start = ((s8[8650752]{0:T(1024)(128)(4,1)}), s8[262144]{0:T(1024)(128)(4,1)S(1)}, s32[]{:S(2)}) async-start(s8[8650752]{0:T(1024)(128)(4,1)} %bitcast.163), calls=%async_computation.6 | async-start | bytes 524288
  102.1 7.5 %slice-start.1 = ((s8[8650752]{0:T(1024)(128)(4,1)}), s8[4194304]{0:T(1024)(128)(4,1)S(1)}, s32[]{:S(2)}) async-start(s8[8650752]{0:T(1024)(128)(4,1)} %bitcast.163), calls=%async_computation.7 | async-start | bytes 8388608
  102.2 7.5 %slice-start.2 = ((s8[8650752]{0:T(1024)(128)(4,1)}), s8[4194304]{0:T(1024)(128)(4,1)S(1)}, s32[]{:S(2)}) async-start(s8[8650752]{0:T(1024)(128)(4,1)} %bitcast.163), calls=%async_computation.8 | async-start | bytes 8388608
  102.2 7.5 %copy-start.6 = (pred[512,1056]{0,1:T(8,128)(4,1)S(1)}, pred[512,1056]{0,1:T(8,128)(4,1)}, u32[]{:S(2)}) copy-start(pred[512,1056]{0,1:T(8,128)(4,1)} %copy-done.4) | copy-start | bytes 1622020
  102.2 7.5 %copy-start.9 = (bf16[1024,1,384]{0,2,1:T(8,128)(2,1)S(1)}, bf16[1024,1,384]{0,2,1:T(8,128)(2,1)}, u32[]{:S(2)}) copy-start(bf16[1024,1,384]{0,2,1:T(8,128)(2,1)} %copy.67) | copy-start | bytes 2359300
  109.7 3.7 %copy-start.8 = (f32[2,512,4]{2,0,1:T(2,128)S(1)}, f32[2,512,4]{2,0,1:T(2,128)}, u32[]{:S(2)}) copy-start(f32[2,512,4]{2,0,1:T(2,128)} %copy.82) | copy-start | bytes 49156
  122.7 13.5 %all-to-all-start.2 = ((f32[16,1,256]{2,1,0:T(1,128)}), f32[16,1,256]{2,1,0:T(1,128)S(1)}, u32[]{:S(2)}, u32[]{:S(2)}) async-start(f32[16,1,256]{2,1,0:T(1,128)} %reshape.134), calls=%async_computation.2 | async-start | bytes 32768 | tf_op jit(solution)/shard_map/all_to_all | solution.py:95
  130.0 12.1 %copy-start.17 = (s32[1,64,1]{1,2,0:T(1,128)S(1)}, s32[1,64,1]{1,2,0:T(1,128)}, u32[]{:S(2)}) copy-start(s32[1,64,1]{1,2,0:T(1,128)} %param.19) | copy-start | bytes 772
  136.2 21.3 %all-to-all-start = ((f32[1,2,512,384]{3,1,0,2:T(2,128)}), f32[1,2,512,384]{3,1,0,2:T(2,128)}, u32[]{:S(2)}, u32[]{:S(2)}) async-start(f32[1,2,512,384]{3,1,0,2:T(2,128)} %maximum_bitcast_fusion), calls=%async_computation | async-start | bytes 3145728 | tf_op jit(solution)/shard_map/all_to_all | solution.py:96
  141.8 106.7 %reduce-scatter.4.cloned.1.call-start = ((), (), s32[]{:S(2)}) async-start(), calls=%async_computation.5 | async-start | bytes 884736
  155.3 4.4 %copy-start.16 = (bf16[2,32,384]{2,1,0:T(8,128)(2,1)S(1)}, bf16[2,32,384]{2,1,0:T(8,128)(2,1)}, u32[]{:S(2)}) copy-start(bf16[2,32,384]{2,1,0:T(8,128)(2,1)} %param.14) | copy-start | bytes 147460
  157.5 1.9 copy-start.2
  159.2 44.5 %copy-start.18 = (f32[3072]{0:T(1024)S(1)}, f32[3072]{0:T(1024)}, u32[]{:S(2)}) copy-start(f32[3072]{0:T(1024)} %param.15) | copy-start | bytes 36868
  202.8 0.9 copy-start.3
Sparse Core Ops, SparseCore 0:
  213.5 34.8 reduce-scatter.3
